TPU v7x, 32 devices: a whole 2x2x4 slice. The times are simulated.
32 devices in a mesh: groups: 2 (over y), row: 16 (over z, x, core).
Axes of the slice: x: 2, y: 2, z: 4, core: 2. Of those that a mesh axis runs over, the one named last changes fastest.
Arguments:
- features: bfloat16 [576, 16384], P(None, ('groups', 'row')), parts along dimension 1, may hold values from -150 to 150
- labels: int32 [16384], P(('groups', 'row')), parts along dimension 0, may hold values 0 or 1
- other_predictor: float32 [16384], P(('groups', 'row')), parts along dimension 0, may hold values from -6 to 6
- coefficients: float32 [8192], P('groups'), parts along dimension 0, may hold values from -0.09375 to 0.09375
- panel_block: int32 [2], P('groups'), parts along dimension 0, may hold values from 0 to 55
Outputs:
- r_factor: float32 [1152, 576], P('groups'), parts along dimension 0
- residual: float32 [16384], P(('groups', 'row')), parts along dimension 0
There are 2 independent parts, one for each index of `groups`. A program takes and returns all parts, laid end to end along the dimension named above; each array names one. Nothing has to cross between parts.
All inputs are finite; a program needn't handle non-finite values. No bound on the sum of `labels` on one device may be relied on, other than what follows from the above.
Results may differ from a plain program's by a relative error of at most 0.0003.
Values sent between devices are 32-bit elements; how exact they have to be, the bound alone decides.
No kernel may reach another device: no remote copies, remote signals or barrier semaphores. Data moves between devices by JAX's collectives and lax.ppermute only.
A program may use at most 64 MiB of HBM per device.

v0:
```python
import math
import jax
import jax.numpy as jnp
from jax import lax
from jax.sharding import PartitionSpec as P

PB = 64
precise = lax.Precision.HIGHEST


def joined(array, axis, combine):
    everything = lax.all_gather(array, axis)
    leading = everything[0]

    def lap(k, so_far):
        return combine(so_far, everything[k])

    return lax.fori_loop(1, lax.axis_size(axis), lap, leading)


def inner_rows(left_rows, right_rows):
    return lax.dot_general(left_rows, right_rows, (((1,), (1,)), ((), ())), precision=precise)


def upper_merge(earlier, another):
    gram_total = jnp.dot(earlier.T, earlier, precision=precise) + jnp.dot(
        another.T, another, precision=precise
    )
    return jnp.linalg.cholesky(gram_total).T


def panel_lower(panel_rows):
    local_gram = inner_rows(panel_rows, panel_rows)
    upper_factor = joined(jnp.linalg.cholesky(local_gram).T, "row", upper_merge)
    return upper_factor.T


def shards(features, labels, other_predictor, coefficients, panel_block):
    window, rows_here = features.shape
    total_rows = rows_here * lax.axis_size("row")
    first_col = panel_block[0] * PB
    window_coef = lax.dynamic_slice(coefficients, (first_col,), (window,))
    as_float = features.astype(jnp.float32)
    linear = jnp.dot(window_coef, as_float, precision=precise) + other_predictor
    fitted = jax.nn.sigmoid(linear)
    weight = jnp.maximum(fitted * (1.0 - fitted), 0.01)
    root_weight = jnp.sqrt(weight)
    norm_scale = 1.0 / math.sqrt(total_rows)
    scaled = as_float * (root_weight * norm_scale)[None, :]
    target = (
        root_weight * linear + (labels.astype(jnp.float32) - fitted) / root_weight
    ) * norm_scale
    working = jnp.concatenate([scaled, target[None, :]], axis=0)
    panels = window // PB
    blocks = []
    for step in range(panels):
        panel_rows = working[:PB]
        trailing = working[PB:]
        lower_factor = panel_lower(panel_rows)
        orthonormal = lax.linalg.triangular_solve(
            lower_factor, panel_rows, left_side=True, lower=True
        )
        coupling = lax.psum(inner_rows(orthonormal, trailing), "row")
        working = trailing - jnp.dot(coupling.T, orthonormal, precision=precise)
        blocks.append(
            jnp.concatenate(
                [jnp.zeros((PB, step * PB), jnp.float32), lower_factor.T, coupling[:, :-1]], axis=1
            )
        )
    return (jnp.concatenate(blocks, axis=0), working[0] * math.sqrt(total_rows))


def solution(mesh):
    in_specs = (
        P(None, ("groups", "row")),
        P(("groups", "row")),
        P(("groups", "row")),
        P("groups"),
        P("groups"),
    )
    out_specs = (P("groups", None), P(("groups", "row")))
    return jax.shard_map(shards, mesh=mesh, in_specs=in_specs, out_specs=out_specs, check_vma=False)
```

profile of v0, /device:TPU:0, one launch (start us, length us, event | category | flops | bytes accessed | tf_op | source)
XLA Modules:
  0.0 2036.4 jit_solution(737754866576527121)
XLA Ops:
  12.4 5.8 cholesky.383
  19.6 24.6 %all-gather = f32[1024,64]{1,0:T(8,128)S(1)} all-gather(f32[64,64]{1,0:T(8,128)S(1)} %copy.89), channel_id=2, replica_groups=mesh['groups'=2,'row'=16] {'row'}, dimensions={0}, use_global_device_ids=true | all-gather | bytes 278528 | tf_op jit(solution)/shard_map/all_gather | solution.py:12
  44.3 116.1 %while.135 = (s32[]{:T(128)}, f32[64,64]{0,1:T(8,128)S(1)}, f32[16,64,64]{2,1,0:T(8,128)S(1)}, s32[]{:T(128)}, s32[]{:T(128)}, /*index=5*/s32[]{:T(128)}) while((s32[]{:T(128)}, f32[64,64]{0,1:T(8,128)S(1)}, f32[16,64,64]{2,1,0:T(8,128)S(1)}, s32[]{:T(128)}, s32[]{:T(128)}, /*index=5*/s32[]{:T(128)}) %tuple.347), condition=%wide.region_3.0_spmd, body=%wide.region_2.0_spmd.sunk | while | flops 6328388 | bytes 246389 | solution.py:18
  44.9 5.8 cholesky.862
  60.3 5.8 cholesky.862
  99.1 5.8 cholesky.862
  114.6 5.8 cholesky.862
  122.3 5.8 cholesky.862
  137.8 5.8 cholesky.862
  145.5 5.8 cholesky.862
  153.3 5.8 cholesky.862
  167.9 86.1 %all-reduce.7.cloned.1.call-done = f32[64,513]{1,0:T(8,128)} async-done(((f32[64,513]{1,0:T(8,128)}), f32[64,513]{1,0:T(8,128)}) %all-reduce.7.cloned.1.call-update) | async-done | bytes 131344 | tf_op jit(solution)/shard_map/psum | solution.py:63
  256.2 5.8 cholesky.394
  263.5 22.8 %all-gather.1 = f32[1024,64]{1,0:T(8,128)S(1)} all-gather(f32[64,64]{1,0:T(8,128)S(1)} %copy.93), channel_id=3, replica_groups=mesh['groups'=2,'row'=16] {'row'}, dimensions={0}, use_global_device_ids=true | all-gather | bytes 278528 | tf_op jit(solution)/shard_map/all_gather | solution.py:12
  286.4 116.1 %while.136 = (s32[]{:T(128)}, f32[64,64]{0,1:T(8,128)S(1)}, f32[16,64,64]{2,1,0:T(8,128)S(1)}, s32[]{:T(128)}, s32[]{:T(128)}, /*index=5*/s32[]{:T(128)}) while((s32[]{:T(128)}, f32[64,64]{0,1:T(8,128)S(1)}, f32[16,64,64]{2,1,0:T(8,128)S(1)}, s32[]{:T(128)}, s32[]{:T(128)}, /*index=5*/s32[]{:T(128)}) %tuple.348), condition=%wide.region_6.9_spmd, body=%wide.region_5.8_spmd.sunk | while | flops 6328388 | bytes 246389 | solution.py:18
  286.9 5.8 cholesky.874
  302.4 5.8 cholesky.874
  310.1 5.8 cholesky.874
  317.9 5.8 cholesky.874
  325.6 5.8 cholesky.874
  333.4 5.8 cholesky.874
  341.1 5.8 cholesky.874
  348.9 5.8 cholesky.874
  356.6 5.8 cholesky.874
  364.3 5.8 cholesky.874
  379.8 5.8 cholesky.874
  410.8 84.3 %all-reduce.9.cloned.1.call-done = f32[64,449]{1,0:T(8,128)} async-done(((f32[64,449]{1,0:T(8,128)}), f32[64,449]{1,0:T(8,128)}) %all-reduce.9.cloned.1.call-update) | async-done | bytes 114960 | tf_op jit(solution)/shard_map/psum | solution.py:63
  504.5 23.4 %all-gather.2 = f32[1024,64]{1,0:T(8,128)S(1)} all-gather(f32[64,64]{1,0:T(8,128)S(1)} %copy.97), channel_id=4, replica_groups=mesh['groups'=2,'row'=16] {'row'}, dimensions={0}, use_global_device_ids=true | all-gather | bytes 278528 | tf_op jit(solution)/shard_map/all_gather | solution.py:12
  528.0 116.1 %while.137 = (s32[]{:T(128)}, f32[64,64]{0,1:T(8,128)S(1)}, f32[16,64,64]{2,1,0:T(8,128)S(1)}, s32[]{:T(128)}, s32[]{:T(128)}, /*index=5*/s32[]{:T(128)}) while((s32[]{:T(128)}, f32[64,64]{0,1:T(8,128)S(1)}, f32[16,64,64]{2,1,0:T(8,128)S(1)}, s32[]{:T(128)}, s32[]{:T(128)}, /*index=5*/s32[]{:T(128)}) %tuple.349), condition=%wide.region_9.12_spmd, body=%wide.region_8.11_spmd.sunk | while | flops 6328388 | bytes 246389 | solution.py:18
  651.8 84.8 %all-reduce.11.cloned.1.call-done = f32[64,385]{1,0:T(8,128)} async-done(((f32[64,385]{1,0:T(8,128)}), f32[64,385]{1,0:T(8,128)}) %all-reduce.11.cloned.1.call-update) | async-done | bytes 98576 | tf_op jit(solution)/shard_map/psum | solution.py:63
  746.0 23.4 %all-gather.3 = f32[1024,64]{1,0:T(8,128)S(1)} all-gather(f32[64,64]{1,0:T(8,128)S(1)} %copy.101), channel_id=5, replica_groups=mesh['groups'=2,'row'=16] {'row'}, dimensions={0}, use_global_device_ids=true | all-gather | bytes 278528 | tf_op jit(solution)/shard_map/all_gather | solution.py:12
  769.5 116.1 %while.138 = (s32[]{:T(128)}, f32[64,64]{0,1:T(8,128)S(1)}, f32[16,64,64]{2,1,0:T(8,128)S(1)}, s32[]{:T(128)}, s32[]{:T(128)}, /*index=5*/s32[]{:T(128)}) while((s32[]{:T(128)}, f32[64,64]{0,1:T(8,128)S(1)}, f32[16,64,64]{2,1,0:T(8,128)S(1)}, s32[]{:T(128)}, s32[]{:T(128)}, /*index=5*/s32[]{:T(128)}) %tuple.350), condition=%wide.region_12.15_spmd, body=%wide.region_11.14_spmd.sunk | while | flops 6328388 | bytes 246389 | solution.py:18
  893.3 85.0 %all-reduce.13.cloned.1.call-done = f32[64,321]{1,0:T(8,128)} async-done(((f32[64,321]{1,0:T(8,128)}), f32[64,321]{1,0:T(8,128)}) %all-reduce.13.cloned.1.call-update) | async-done | bytes 82192 | tf_op jit(solution)/shard_map/psum | solution.py:63
  987.6 20.8 %all-gather.4 = f32[1024,64]{1,0:T(8,128)S(1)} all-gather(f32[64,64]{1,0:T(8,128)S(1)} %copy.105), channel_id=6, replica_groups=mesh['groups'=2,'row'=16] {'row'}, dimensions={0}, use_global_device_ids=true | all-gather | bytes 278528 | tf_op jit(solution)/shard_map/all_gather | solution.py:12
  1008.5 116.1 %while.139 = (s32[]{:T(128)}, f32[64,64]{0,1:T(8,128)S(1)}, f32[16,64,64]{2,1,0:T(8,128)S(1)}, s32[]{:T(128)}, s32[]{:T(128)}, /*index=5*/s32[]{:T(128)}) while((s32[]{:T(128)}, f32[64,64]{0,1:T(8,128)S(1)}, f32[16,64,64]{2,1,0:T(8,128)S(1)}, s32[]{:T(128)}, s32[]{:T(128)}, /*index=5*/s32[]{:T(128)}) %tuple.351), condition=%wide.region_15.18_spmd, body=%wide.region_14.17_spmd.sunk | while | flops 6328388 | bytes 246389 | solution.py:18
  1132.1 85.3 %all-reduce.15.cloned.1.call-done = f32[64,257]{1,0:T(8,128)} async-done(((f32[64,257]{1,0:T(8,128)}), f32[64,257]{1,0:T(8,128)}) %all-reduce.15.cloned.1.call-update) | async-done | bytes 65808 | tf_op jit(solution)/shard_map/psum | solution.py:63
  1226.6 20.8 %all-gather.5 = f32[1024,64]{1,0:T(8,128)S(1)} all-gather(f32[64,64]{1,0:T(8,128)S(1)} %copy.109), channel_id=7, replica_groups=mesh['groups'=2,'row'=16] {'row'}, dimensions={0}, use_global_device_ids=true | all-gather | bytes 278528 | tf_op jit(solution)/shard_map/all_gather | solution.py:12
  1247.5 116.1 %while.140 = (s32[]{:T(128)}, f32[64,64]{0,1:T(8,128)S(1)}, f32[16,64,64]{2,1,0:T(8,128)S(1)}, s32[]{:T(128)}, s32[]{:T(128)}, /*index=5*/s32[]{:T(128)}) while((s32[]{:T(128)}, f32[64,64]{0,1:T(8,128)S(1)}, f32[16,64,64]{2,1,0:T(8,128)S(1)}, s32[]{:T(128)}, s32[]{:T(128)}, /*index=5*/s32[]{:T(128)}) %tuple.352), condition=%wide.region_18.21_spmd, body=%wide.region_17.20_spmd.sunk | while | flops 6328388 | bytes 246389 | solution.py:18
  1369.4 57.9 %psum.68 = f32[64,193]{1,0:T(8,128)S(1)} all-reduce(f32[64,193]{1,0:T(8,128)S(1)} %fusion.46), channel_id=1, replica_groups=mesh['groups'=2,'row'=16] {'row'}, use_global_device_ids=true, to_apply=%region_19.22 | all-reduce | flops 12352 | bytes 98816 | tf_op jit(solution)/shard_map/psum | solution.py:63
  1435.5 18.9 all-gather.6
  1454.5 116.1 %while.141 = (s32[]{:T(128)}, f32[64,64]{0,1:T(8,128)S(1)}, f32[16,64,64]{2,1,0:T(8,128)S(1)}, s32[]{:T(128)}, s32[]{:T(128)}, /*index=5*/s32[]{:T(128)}) while((s32[]{:T(128)}, f32[64,64]{0,1:T(8,128)S(1)}, f32[16,64,64]{2,1,0:T(8,128)S(1)}, s32[]{:T(128)}, s32[]{:T(128)}, /*index=5*/s32[]{:T(128)}) %tuple.353), condition=%wide.region_21.24_spmd, body=%wide.region_20.23_spmd.sunk | while | flops 6328388 | bytes 246389 | solution.py:18
  1576.3 59.9 %psum.69 = f32[64,129]{1,0:T(8,128)S(1)} all-reduce(f32[64,129]{1,0:T(8,128)S(1)} %fusion.48), channel_id=1, replica_groups=mesh['groups'=2,'row'=16] {'row'}, use_global_device_ids=true, to_apply=%region_22.25 | all-reduce | flops 8256 | bytes 66048 | tf_op jit(solution)/shard_map/psum | solution.py:63
  1644.3 18.7 all-gather.7
  1663.1 116.1 %while.142 = (s32[]{:T(128)}, f32[64,64]{0,1:T(8,128)S(1)}, f32[16,64,64]{2,1,0:T(8,128)S(1)}, s32[]{:T(128)}, s32[]{:T(128)}, /*index=5*/s32[]{:T(128)}) while((s32[]{:T(128)}, f32[64,64]{0,1:T(8,128)S(1)}, f32[16,64,64]{2,1,0:T(8,128)S(1)}, s32[]{:T(128)}, s32[]{:T(128)}, /*index=5*/s32[]{:T(128)}) %tuple.354), condition=%wide.region_24.27_spmd, body=%wide.region_23.26_spmd.sunk | while | flops 6328388 | bytes 246389 | solution.py:18
  1784.7 59.9 %psum.70 = f32[64,65]{1,0:T(8,128)S(1)} all-reduce(f32[64,65]{1,0:T(8,128)S(1)} %fusion.50), channel_id=1, replica_groups=mesh['groups'=2,'row'=16] {'row'}, use_global_device_ids=true, to_apply=%region_25.28 | all-reduce | flops 4160 | bytes 33280 | tf_op jit(solution)/shard_map/psum | solution.py:63
  1852.6 18.7 all-gather.8
  1871.3 116.1 %while.143 = (s32[]{:T(128)}, f32[64,64]{0,1:T(8,128)S(1)}, f32[16,64,64]{2,1,0:T(8,128)S(1)}, s32[]{:T(128)}, s32[]{:T(128)}, /*index=5*/s32[]{:T(128)}) while((s32[]{:T(128)}, f32[64,64]{0,1:T(8,128)S(1)}, f32[16,64,64]{2,1,0:T(8,128)S(1)}, s32[]{:T(128)}, s32[]{:T(128)}, /*index=5*/s32[]{:T(128)}) %tuple.346), condition=%wide.region_27.30_spmd, body=%wide.region_26.29_spmd.sunk | while | flops 6328388 | bytes 246389 | solution.py:18
  1993.3 31.9 %psum.71 = f32[64]{0:T(128)S(1)} all-reduce(f32[64]{0:T(128)S(1)} %convolution_bitcast_fusion), channel_id=1, replica_groups=mesh['groups'=2,'row'=16] {'row'}, use_global_device_ids=true, to_apply=%region_28.31 | all-reduce | flops 64 | bytes 512 | tf_op jit(solution)/shard_map/psum | solution.py:63
  (1254 shorter events, 1063.1 us)
Async XLA Ops:
  7.2 246.8 %all-reduce.7.cloned.1.call-start = ((), (), s32[]{:S(2)}) async-start(), calls=%async_computation | async-start | bytes 327680 | tf_op jit(solution)/shard_map/psum | solution.py:63
  167.6 327.4 %all-reduce.9.cloned.1.call-start = ((), (), s32[]{:S(2)}) async-start(), calls=%async_computation.1 | async-start | bytes 262144 | tf_op jit(solution)/shard_map/psum | solution.py:63
  402.5 7.4 slice-start
  409.4 327.2 %all-reduce.11.cloned.1.call-start = ((), (), s32[]{:S(2)}) async-start(), calls=%async_computation.2 | async-start | bytes 262144 | tf_op jit(solution)/shard_map/psum | solution.py:63
  644.1 6.8 copy-start
  650.9 327.4 %all-reduce.13.cloned.1.call-start = ((), (), s32[]{:S(2)}) async-start(), calls=%async_computation.3 | async-start | bytes 196608 | tf_op jit(solution)/shard_map/psum | solution.py:63
  885.6 6.8 slice-start.2
  892.2 325.2 %all-reduce.15.cloned.1.call-start = ((), (), s32[]{:S(2)}) async-start(), calls=%async_computation.4 | async-start | bytes 196608 | tf_op jit(solution)/shard_map/psum | solution.py:63
  1124.6 6.6 copy-start.2
  1636.2 351.5 %copy-start.1 = (f32[64,129]{1,0:T(8,128)}, f32[64,129]{1,0:T(8,128)S(1)}, u32[]{:S(2)}) copy-start(f32[64,129]{1,0:T(8,128)S(1)} %psum.69) | copy-start | bytes 99076
  1871.3 154.6 %slice-start.3 = ((f32[64,257]{1,0:T(8,128)}), f32[64,256]{1,0:T(8,128)S(1)}, s32[]{:S(2)}) async-start(f32[64,257]{1,0:T(8,128)} %all-reduce.15.cloned.1.call-done), calls=%async_computation.8 | async-start | bytes 131072 | tf_op jit(solution)/shard_map/slice | solution.py:67
  1987.7 39.7 %slice-start.1 = ((f32[64,129]{1,0:T(8,128)}), f32[64,128]{1,0:T(8,128)S(1)}, s32[]{:S(2)}) async-start(f32[64,129]{1,0:T(8,128)} %copy-done.1), calls=%async_computation.6 | async-start | bytes 65536 | tf_op jit(solution)/shard_map/slice | solution.py:67
Sparse Core Ops, SparseCore 0:
  167.7 86.1 all-reduce.6
  409.5 85.4 all-reduce.8
  651.0 85.5 all-reduce.10
  892.4 85.9 all-reduce.12
  1131.4 85.9 all-reduce.14
where the time goes:
time: 2050 us; the launch traced here: 2040 us
  other arithmetic  1090 us (53%)
  waiting for transfers between devices  426 us (21%)
  blocking collectives  402 us (20%)
  matrix products  84.3 us (4%)
    another operation x405, other arithmetic, upper_merge(): return jnp.linalg.cholesky(gram_total).T  880 us
    psum x5, waiting for transfers between devices, shards(): coupling = lax.psum(inner_rows(orthonormal, trailing), 'row')  425 us
    psum x4, blocking collectives, shards(): coupling = lax.psum(inner_rows(orthonormal, trailing), 'row')  210 us
    all_gather x9, blocking collectives, joined(): everything = lax.all_gather(array, axis)  192 us
    transpose x135, other arithmetic, upper_merge(): return jnp.linalg.cholesky(gram_total).T  88 us
    another operation x27, other arithmetic, panel_lower(): upper_factor = joined(jnp.linalg.cholesky(local_gram).T, 'row', upper_merge)  58.7 us
    another operation x18, other arithmetic, shards(): lax.linalg.triangular_solve(lower_factor, panel_rows, left_side=True, low...  44.2 us
  transfers between devices with their start and end apart: 5, of which 5 were waited for; matrix products, arithmetic and copies ran while one was open for 0% of the time, Pallas kernels for 0%

commit v1 on v0

--- a/solution.py
+++ b/solution.py
@@ -60,7 +60,7 @@
         orthonormal = lax.linalg.triangular_solve(
             lower_factor, panel_rows, left_side=True, lower=True
         )
-        coupling = lax.psum(inner_rows(orthonormal, trailing), "row")
+        coupling = jnp.sum(lax.all_gather(inner_rows(orthonormal, trailing), "row"), axis=0)
         working = trailing - jnp.dot(coupling.T, orthonormal, precision=precise)
         blocks.append(
             jnp.concatenate(

time: 2050 us -> 1690 us (0.82)
  waiting for transfers between devices: 426 us -> 189 us
  blocking collectives: 402 us -> 282 us
    psum x5 -> x0, waiting for transfers between devices: 425 us -> none  [shards(): coupling = lax.psum(inner_rows(orthonormal, trailing), 'row')]
    psum x4 -> x0, blocking collectives: 210 us -> none  [shards(): coupling = lax.psum(inner_rows(orthonormal, trailing), 'row')]
    all_gather x0 -> x5, waiting for transfers between devices: none -> 189 us  [shards(): lax.all_gather(inner_rows(orthonormal, trailing), 'row')]
    all_gather x0 -> x3, blocking collectives: none -> 60.7 us  [shards(): lax.all_gather(inner_rows(orthonormal, trailing), 'row')]
    unnamed x0 -> x1, blocking collectives: none -> 29.8 us
where the time goes in v1:
time: 1690 us; the launch traced here: 1680 us
  other arithmetic  1090 us (64%)
  blocking collectives  282 us (17%)
  waiting for transfers between devices  189 us (11%)
  matrix products  79.9 us (5%)
    another operation x405, other arithmetic, upper_merge(): return jnp.linalg.cholesky(gram_total).T  880 us
    all_gather x9, blocking collectives, joined(): everything = lax.all_gather(array, axis)  191 us
    all_gather x5, waiting for transfers between devices, shards(): lax.all_gather(inner_rows(orthonormal, trailing), 'row')  189 us
    transpose x135, other arithmetic, upper_merge(): return jnp.linalg.cholesky(gram_total).T  88 us
    all_gather x3, blocking collectives, shards(): lax.all_gather(inner_rows(orthonormal, trailing), 'row')  60.7 us
    another operation x27, other arithmetic, panel_lower(): upper_factor = joined(jnp.linalg.cholesky(local_gram).T, 'row', upper_merge)  58.8 us
    another operation x18, other arithmetic, shards(): lax.linalg.triangular_solve(lower_factor, panel_rows, left_side=True, low...  44.1 us
  transfers between devices with their start and end apart: 5, of which 5 were waited for; matrix products, arithmetic and copies ran while one was open for 0% of the time, Pallas kernels for 0%

profile of v1, /device:TPU:0, one launch (start us, length us, event | category | flops | bytes accessed | tf_op | source)
XLA Modules:
  0.0 1683.4 jit_solution(14957985581196737208)
XLA Ops:
  12.4 5.8 cholesky.383
  19.6 24.6 %all-gather = f32[1024,64]{1,0:T(8,128)S(1)} all-gather(f32[64,64]{1,0:T(8,128)S(1)} %copy.152), channel_id=2, replica_groups=mesh['groups'=2,'row'=16] {'row'}, dimensions={0}, use_global_device_ids=true | all-gather | bytes 278528 | tf_op jit(solution)/shard_map/all_gather | solution.py:12
  44.3 116.1 %while.135 = (s32[]{:T(128)}, f32[64,64]{0,1:T(8,128)S(1)}, f32[16,64,64]{2,1,0:T(8,128)S(1)}, s32[]{:T(128)}, s32[]{:T(128)}, /*index=5*/s32[]{:T(128)}) while((s32[]{:T(128)}, f32[64,64]{0,1:T(8,128)S(1)}, f32[16,64,64]{2,1,0:T(8,128)S(1)}, s32[]{:T(128)}, s32[]{:T(128)}, /*index=5*/s32[]{:T(128)}) %tuple.356), condition=%wide.region_3.0_spmd, body=%wide.region_2.0_spmd.sunk | while | flops 6328388 | bytes 246389 | solution.py:18
  44.9 5.8 cholesky.862
  52.6 5.8 cholesky.862
  60.3 5.8 cholesky.862
  68.1 5.8 cholesky.862
  75.8 5.8 cholesky.862
  83.6 5.8 cholesky.862
  91.3 5.8 cholesky.862
  106.8 5.8 cholesky.862
  145.5 5.8 cholesky.862
  153.3 5.8 cholesky.862
  167.7 40.5 %all-gather.24.cloned.1.call-done = f32[1024,513]{1,0:T(8,128)} async-done(((f32[64,513]{1,0:T(8,128)}), f32[1024,513]{1,0:T(8,128)}) %all-gather.24.cloned.1.call-update) | async-done | bytes 2101264 | tf_op jit(solution)/shard_map/all_gather | solution.py:63
  211.4 5.8 cholesky.394
  218.7 20.7 %all-gather.2 = f32[1024,64]{1,0:T(8,128)S(1)} all-gather(f32[64,64]{1,0:T(8,128)S(1)} %copy.156), channel_id=4, replica_groups=mesh['groups'=2,'row'=16] {'row'}, dimensions={0}, use_global_device_ids=true | all-gather | bytes 278528 | tf_op jit(solution)/shard_map/all_gather | solution.py:12
  239.4 116.1 %while.136 = (s32[]{:T(128)}, f32[64,64]{0,1:T(8,128)S(1)}, f32[16,64,64]{2,1,0:T(8,128)S(1)}, s32[]{:T(128)}, s32[]{:T(128)}, /*index=5*/s32[]{:T(128)}) while((s32[]{:T(128)}, f32[64,64]{0,1:T(8,128)S(1)}, f32[16,64,64]{2,1,0:T(8,128)S(1)}, s32[]{:T(128)}, s32[]{:T(128)}, /*index=5*/s32[]{:T(128)}) %tuple.357), condition=%wide.region_6.9_spmd, body=%wide.region_5.8_spmd.sunk | while | flops 6328388 | bytes 246389 | solution.py:18
  240.0 5.8 cholesky.874
  247.7 5.8 cholesky.874
  255.5 5.8 cholesky.874
  271.0 5.8 cholesky.874
  278.7 5.8 cholesky.874
  286.5 5.8 cholesky.874
  294.2 5.8 cholesky.874
  301.9 5.8 cholesky.874
  309.7 5.8 cholesky.874
  362.7 38.6 %all-gather.26.cloned.1.call-done = f32[1024,449]{1,0:T(8,128)} async-done(((f32[64,449]{1,0:T(8,128)}), f32[1024,449]{1,0:T(8,128)}) %all-gather.26.cloned.1.call-update) | async-done | bytes 1839120 | tf_op jit(solution)/shard_map/all_gather | solution.py:63
  411.6 20.6 %all-gather.4 = f32[1024,64]{1,0:T(8,128)S(1)} all-gather(f32[64,64]{1,0:T(8,128)S(1)} %copy.160), channel_id=6, replica_groups=mesh['groups'=2,'row'=16] {'row'}, dimensions={0}, use_global_device_ids=true | all-gather | bytes 278528 | tf_op jit(solution)/shard_map/all_gather | solution.py:12
  432.3 116.1 %while.137 = (s32[]{:T(128)}, f32[64,64]{0,1:T(8,128)S(1)}, f32[16,64,64]{2,1,0:T(8,128)S(1)}, s32[]{:T(128)}, s32[]{:T(128)}, /*index=5*/s32[]{:T(128)}) while((s32[]{:T(128)}, f32[64,64]{0,1:T(8,128)S(1)}, f32[16,64,64]{2,1,0:T(8,128)S(1)}, s32[]{:T(128)}, s32[]{:T(128)}, /*index=5*/s32[]{:T(128)}) %tuple.358), condition=%wide.region_9.12_spmd, body=%wide.region_8.11_spmd.sunk | while | flops 6328388 | bytes 246389 | solution.py:18
  555.3 38.8 %all-gather.28.cloned.1.call-done = f32[1024,385]{1,0:T(8,128)} async-done(((f32[64,385]{1,0:T(8,128)}), f32[1024,385]{1,0:T(8,128)}) %all-gather.28.cloned.1.call-update) | async-done | bytes 1576976 | tf_op jit(solution)/shard_map/all_gather | solution.py:63
  604.3 20.6 %all-gather.6 = f32[1024,64]{1,0:T(8,128)S(1)} all-gather(f32[64,64]{1,0:T(8,128)S(1)} %copy.164), channel_id=8, replica_groups=mesh['groups'=2,'row'=16] {'row'}, dimensions={0}, use_global_device_ids=true | all-gather | bytes 278528 | tf_op jit(solution)/shard_map/all_gather | solution.py:12
  625.0 116.1 %while.138 = (s32[]{:T(128)}, f32[64,64]{0,1:T(8,128)S(1)}, f32[16,64,64]{2,1,0:T(8,128)S(1)}, s32[]{:T(128)}, s32[]{:T(128)}, /*index=5*/s32[]{:T(128)}) while((s32[]{:T(128)}, f32[64,64]{0,1:T(8,128)S(1)}, f32[16,64,64]{2,1,0:T(8,128)S(1)}, s32[]{:T(128)}, s32[]{:T(128)}, /*index=5*/s32[]{:T(128)}) %tuple.359), condition=%wide.region_12.15_spmd, body=%wide.region_11.14_spmd.sunk | while | flops 6328388 | bytes 246389 | solution.py:18
  748.0 36.7 %all-gather.30.cloned.1.call-done = f32[1024,321]{1,0:T(8,128)} async-done(((f32[64,321]{1,0:T(8,128)}), f32[1024,321]{1,0:T(8,128)}) %all-gather.30.cloned.1.call-update) | async-done | bytes 1314832 | tf_op jit(solution)/shard_map/all_gather | solution.py:63
  794.6 20.5 %all-gather.8 = f32[1024,64]{1,0:T(8,128)S(1)} all-gather(f32[64,64]{1,0:T(8,128)S(1)} %copy.168), channel_id=10, replica_groups=mesh['groups'=2,'row'=16] {'row'}, dimensions={0}, use_global_device_ids=true | all-gather | bytes 278528 | tf_op jit(solution)/shard_map/all_gather | solution.py:12
  815.2 116.1 %while.139 = (s32[]{:T(128)}, f32[64,64]{0,1:T(8,128)S(1)}, f32[16,64,64]{2,1,0:T(8,128)S(1)}, s32[]{:T(128)}, s32[]{:T(128)}, /*index=5*/s32[]{:T(128)}) while((s32[]{:T(128)}, f32[64,64]{0,1:T(8,128)S(1)}, f32[16,64,64]{2,1,0:T(8,128)S(1)}, s32[]{:T(128)}, s32[]{:T(128)}, /*index=5*/s32[]{:T(128)}) %tuple.360), condition=%wide.region_15.18_spmd, body=%wide.region_14.17_spmd.sunk | while | flops 6328388 | bytes 246389 | solution.py:18
  940.2 34.8 %all-gather.32.cloned.1.call-done = f32[1024,257]{1,0:T(8,128)} async-done(((f32[64,257]{1,0:T(8,128)}), f32[1024,257]{1,0:T(8,128)}) %all-gather.32.cloned.1.call-update) | async-done | bytes 1052688 | tf_op jit(solution)/shard_map/all_gather | solution.py:63
  984.9 20.6 %all-gather.10 = f32[1024,64]{1,0:T(8,128)S(1)} all-gather(f32[64,64]{1,0:T(8,128)S(1)} %copy.172), channel_id=12, replica_groups=mesh['groups'=2,'row'=16] {'row'}, dimensions={0}, use_global_device_ids=true | all-gather | bytes 278528 | tf_op jit(solution)/shard_map/all_gather | solution.py:12
  1005.5 116.1 %while.140 = (s32[]{:T(128)}, f32[64,64]{0,1:T(8,128)S(1)}, f32[16,64,64]{2,1,0:T(8,128)S(1)}, s32[]{:T(128)}, s32[]{:T(128)}, /*index=5*/s32[]{:T(128)}) while((s32[]{:T(128)}, f32[64,64]{0,1:T(8,128)S(1)}, f32[16,64,64]{2,1,0:T(8,128)S(1)}, s32[]{:T(128)}, s32[]{:T(128)}, /*index=5*/s32[]{:T(128)}) %tuple.361), condition=%wide.region_18.21_spmd, body=%wide.region_17.20_spmd.sunk | while | flops 6328388 | bytes 246389 | solution.py:18
  1127.5 21.1 %all-gather.11 = f32[1024,193]{1,0:T(8,128)S(1)} all-gather(f32[64,193]{1,0:T(8,128)S(1)} %fusion.46), channel_id=13, replica_groups=mesh['groups'=2,'row'=16] {'row'}, dimensions={0}, use_global_device_ids=true | all-gather | bytes 839936 | tf_op jit(solution)/shard_map/all_gather | solution.py:63
  1156.8 21.9 %all-gather.12 = f32[1024,64]{1,0:T(8,128)S(1)} all-gather(f32[64,64]{1,0:T(8,128)S(1)} %copy.176), channel_id=14, replica_groups=mesh['groups'=2,'row'=16] {'row'}, dimensions={0}, use_global_device_ids=true | all-gather | bytes 278528 | tf_op jit(solution)/shard_map/all_gather | solution.py:12
  1178.8 116.1 %while.141 = (s32[]{:T(128)}, f32[64,64]{0,1:T(8,128)S(1)}, f32[16,64,64]{2,1,0:T(8,128)S(1)}, s32[]{:T(128)}, s32[]{:T(128)}, /*index=5*/s32[]{:T(128)}) while((s32[]{:T(128)}, f32[64,64]{0,1:T(8,128)S(1)}, f32[16,64,64]{2,1,0:T(8,128)S(1)}, s32[]{:T(128)}, s32[]{:T(128)}, /*index=5*/s32[]{:T(128)}) %tuple.362), condition=%wide.region_21.24_spmd, body=%wide.region_20.23_spmd.sunk | while | flops 6328388 | bytes 246389 | solution.py:18
  1300.6 20.7 %all-gather.13 = f32[1024,129]{1,0:T(8,128)S(1)} all-gather(f32[64,129]{1,0:T(8,128)S(1)} %fusion.48), channel_id=15, replica_groups=mesh['groups'=2,'row'=16] {'row'}, dimensions={0}, use_global_device_ids=true | all-gather | bytes 561408 | tf_op jit(solution)/shard_map/all_gather | solution.py:63
  1329.5 21.1 %all-gather.14 = f32[1024,64]{1,0:T(8,128)S(1)} all-gather(f32[64,64]{1,0:T(8,128)S(1)} %copy.180), channel_id=16, replica_groups=mesh['groups'=2,'row'=16] {'row'}, dimensions={0}, use_global_device_ids=true | all-gather | bytes 278528 | tf_op jit(solution)/shard_map/all_gather | solution.py:12
  1350.6 116.1 %while.142 = (s32[]{:T(128)}, f32[64,64]{0,1:T(8,128)S(1)}, f32[16,64,64]{2,1,0:T(8,128)S(1)}, s32[]{:T(128)}, s32[]{:T(128)}, /*index=5*/s32[]{:T(128)}) while((s32[]{:T(128)}, f32[64,64]{0,1:T(8,128)S(1)}, f32[16,64,64]{2,1,0:T(8,128)S(1)}, s32[]{:T(128)}, s32[]{:T(128)}, /*index=5*/s32[]{:T(128)}) %tuple.363), condition=%wide.region_24.27_spmd, body=%wide.region_23.26_spmd.sunk | while | flops 6328388 | bytes 246389 | solution.py:18
  1472.3 18.9 %all-gather.15 = f32[1024,65]{1,0:T(8,128)S(1)} all-gather(f32[64,65]{1,0:T(8,128)S(1)} %fusion.50), channel_id=17, replica_groups=mesh['groups'=2,'row'=16] {'row'}, dimensions={0}, use_global_device_ids=true | all-gather | bytes 282880 | tf_op jit(solution)/shard_map/all_gather | solution.py:63
  1499.2 20.6 %all-gather.16 = f32[1024,64]{1,0:T(8,128)S(1)} all-gather(f32[64,64]{1,0:T(8,128)S(1)} %copy.184), channel_id=18, replica_groups=mesh['groups'=2,'row'=16] {'row'}, dimensions={0}, use_global_device_ids=true | all-gather | bytes 278528 | tf_op jit(solution)/shard_map/all_gather | solution.py:12
  1519.8 116.1 %while.143 = (s32[]{:T(128)}, f32[64,64]{0,1:T(8,128)S(1)}, f32[16,64,64]{2,1,0:T(8,128)S(1)}, s32[]{:T(128)}, s32[]{:T(128)}, /*index=5*/s32[]{:T(128)}) while((s32[]{:T(128)}, f32[64,64]{0,1:T(8,128)S(1)}, f32[16,64,64]{2,1,0:T(8,128)S(1)}, s32[]{:T(128)}, s32[]{:T(128)}, /*index=5*/s32[]{:T(128)}) %tuple.355), condition=%wide.region_27.30_spmd, body=%wide.region_26.29_spmd.sunk | while | flops 6328388 | bytes 246389 | solution.py:18
  1642.0 29.8 %all-reduce.1 = f32[1024]{0:T(1024)S(1)} all-reduce(f32[1024]{0:T(1024)S(1)} %dynamic-update-slice.2), channel_id=19, replica_groups=mesh['groups'=2,'row'=16] {'row'}, use_global_device_ids=true, to_apply=%add.1 | all-reduce | flops 1024 | bytes 8192
  (1261 shorter events, 1065.4 us)
Async XLA Ops:
  7.2 200.9 %all-gather.24.cloned.1.call-start = ((), (), s32[]{:S(2)}) async-start(), calls=%async_computation | async-start | bytes 2785280 | tf_op jit(solution)/shard_map/all_gather | solution.py:63
  167.6 233.7 %all-gather.26.cloned.1.call-start = ((), (), s32[]{:S(2)}) async-start(), calls=%async_computation.1 | async-start | bytes 2228224 | tf_op jit(solution)/shard_map/all_gather | solution.py:63
  362.5 231.6 %all-gather.28.cloned.1.call-start = ((), (), s32[]{:S(2)}) async-start(), calls=%async_computation.2 | async-start | bytes 2228224 | tf_op jit(solution)/shard_map/all_gather | solution.py:63
  555.2 229.5 %all-gather.30.cloned.1.call-start = ((), (), s32[]{:S(2)}) async-start(), calls=%async_computation.3 | async-start | bytes 1671168 | tf_op jit(solution)/shard_map/all_gather | solution.py:63
  747.7 227.3 %all-gather.32.cloned.1.call-start = ((), (), s32[]{:S(2)}) async-start(), calls=%async_computation.4 | async-start | bytes 1671168 | tf_op jit(solution)/shard_map/all_gather | solution.py:63
  815.2 123.0 %copy-start.1 = (u32[32]{0:T(128)S(1)}, u32[32]{0:T(128)}, u32[]{:S(2)}) copy-start(u32[32]{0:T(128)} %constant.375) | copy-start | bytes 388
  940.2 186.7 %copy-start = (f32[576,576]{1,0:T(8,128)}, f32[576,576]{1,0:T(8,128)S(1)}, u32[]{:S(2)}) copy-start(f32[576,576]{1,0:T(8,128)S(1)} %maximum_dynamic-update-slice_fusion.4) | copy-start | bytes 3981316
Sparse Core Ops, SparseCore 0:
  167.7 40.3 all-gather.23
  362.6 38.6 all-gather.25
  555.3 38.6 all-gather.27
  747.9 36.8 all-gather.29
  938.1 36.8 all-gather.31
